TPU v7x, 512 devices: a whole 4x4x16 slice. The times are simulated.
512 devices in a mesh: dp: 8 (over z_lo), seq: 4 (over z_hi, core), expert: 16 (over x, y).
Axes of the slice: x: 4, y: 4, z: 16 (z_hi: 2, z_lo: 8; z = z_hi * 8 + z_lo), core: 2. Of those that a mesh axis runs over, the one named last changes fastest.
Arguments:
- keys: bfloat16 [16, 4096, 512], P('expert', ('dp', 'seq')), may hold values from -4 to 4
- values: bfloat16 [16, 4096, 512], P('expert', ('dp', 'seq')), may hold values from -5 to 5
- queries: bfloat16 [16, 32, 4096], P('expert', ('dp', 'seq')), may hold values from -80 to 80
- residual: bfloat16 [16, 32, 2048], P('expert', ('dp', 'seq')), may hold values from -9 to 9
- out_proj: bfloat16 [4096, 2048], P(('dp', 'seq')), may hold values from -0.09375 to 0.09375
- norm_gain: bfloat16 [2048], replicated, may hold values from 0.25 to 1.75
- router: bfloat16 [2048, 128], replicated, may hold values from -8 to 8
- w_gate: bfloat16 [128, 2048, 768], P(('dp', 'expert'), None, 'seq'), may hold values from -0.125 to 0.125
- w_up: bfloat16 [128, 2048, 768], P(('dp', 'expert'), None, 'seq'), may hold values from -0.125 to 0.125
- w_down: bfloat16 [128, 768, 2048], P(('dp', 'expert'), 'seq'), may hold values from -0.21875 to 0.21875
- head_vec: bfloat16 [2048], replicated, may hold values from -0.09 to 0.09
- routes: int32 [16, 32, 8], P('expert', 'dp'), may hold values from 0 to 127, all different within a row; in each aligned block of 4 rows (0 to 3, 4 to 7, ..., all dimensions but the last counted through in order) at most 2 rows name the same one
- step_pos: int32 [16, 32], P('expert'), may hold values from 0 to 4095, as said below
- labels: int32 [16, 32], P('expert', ('dp', 'seq')), may hold values 0 or 1
- trace_len: int32 [16, 8], P('expert'), may hold values from 1 to 1024, 4096 in all within a row
Outputs:
- loss: float32 [], replicated
- grad_down: bfloat16 [128, 768, 2048], P(('dp', 'expert'), 'seq')
- grad_router: bfloat16 [2048, 128], P(('dp', 'seq', 'expert'))
Inputs may be any that keep to these rules, and one draw needn't show every extreme that they name: `step_pos`: increasing along each pack; distinct. `routes`: in each aligned block of 4 step ends (those of one index of dp in one pack) no expert is named by more than 2 of them.
All inputs are finite; a program needn't handle non-finite values. No bound on the sum of `labels` on one device may be relied on, other than what follows from the above.
Results may differ from a plain program's by a relative error of at most 0.018.
Values may be sent and summed in bfloat16 or wider, within the bound.
No kernel may reach another device: no remote copies, remote signals or barrier semaphores. Data moves between devices by JAX's collectives and lax.ppermute only.
A program may use at most 64 MiB of HBM per device.

v0:
```python
import jax
import jax.numpy as jnp
from jax import lax
from jax.sharding import Mesh
from jax.sharding import PartitionSpec as P

QUERY_HEADS = 32
KEY_VALUE_HEADS = 4
HEAD_WIDTH = 128
DP_EXPERT = ("dp", "expert_0", "expert_1")
DP_SEQ = ("dp", "seq_0", "seq_1")
SEQ = ("seq_0", "seq_1")
DP_SEQ_EXPERT = ("dp", "seq_0", "seq_1", "expert_0", "expert_1")
EXPERT = ("expert_0", "expert_1")
ROWS = DP_SEQ_EXPERT
MASKED = -1e30
EPSILON = 1e-06


def joined_along(blocks, dim):
    blocks = jnp.moveaxis(blocks, 0, dim)
    lengths = blocks.shape
    return blocks.reshape(*lengths[:dim], lengths[dim] * lengths[dim + 1], *lengths[dim + 2 :])


def from_everyone(array, axis):
    copies = jnp.broadcast_to(array, (lax.axis_size(axis), *array.shape))
    return lax.all_to_all(copies, axis, split_axis=0, concat_axis=0, tiled=True)


def gather_directly(array, axis, dim):
    return joined_along(from_everyone(array, axis), dim)


def in_blocks(array, dim, count):
    lengths = array.shape
    blocks = array.reshape(*lengths[:dim], count, lengths[dim] // count, *lengths[dim + 1 :])
    return jnp.moveaxis(blocks, dim, 0)


def sent_and_summed(array, axis, dim):
    count = lax.axis_size(axis)
    blocks = lax.all_to_all(in_blocks(array, dim, count), axis, 0, 0, tiled=True)
    return jnp.sum(blocks.astype(jnp.float32), axis=0)


def rms_scale(stream):
    return lax.rsqrt(jnp.mean(stream * stream, axis=-1, keepdims=True) + EPSILON)


def head_logit(final, head_vec):
    return jnp.sum(final * rms_scale(final) * head_vec.astype(jnp.float32)[None, :], axis=1)


def split_pair(value):
    high = value.astype(jnp.bfloat16)
    low = (value - high.astype(jnp.float32)).astype(jnp.bfloat16)
    return (high, low)


def join_pair(high, low):
    return high.astype(jnp.float32) + low.astype(jnp.float32)


def merge_heads(weighted_r, totals_r, peak_r):
    peak_all = jnp.max(peak_r, axis=0)
    factor = jnp.exp(peak_r - peak_all[None])
    weighted_sum = jnp.sum(weighted_r * factor[..., None], axis=0)
    totals_sum = jnp.sum(totals_r * factor, axis=0)
    merged = weighted_sum / totals_sum[..., None]
    return merged.reshape(merged.shape[0], -1).astype(jnp.bfloat16)


def shards(
    keys,
    values,
    queries,
    residual,
    out_proj,
    norm_gain,
    router,
    w_gate,
    w_up,
    w_down,
    head_vec,
    routes,
    step_pos,
    labels,
    trace_len,
):
    block_routes = lax.all_gather(routes[0], DP_EXPERT, axis=0)
    block_routes = block_routes.reshape(
        lax.axis_size("dp"), lax.axis_size(EXPERT), *routes.shape[1:]
    )
    routes_all = jnp.swapaxes(block_routes, 1, 2).reshape(-1, routes.shape[2])
    count_of_keys = keys.shape[1]
    query_groups = QUERY_HEADS // KEY_VALUE_HEADS
    query_all = gather_directly(queries, DP_SEQ, 1)[0]
    positions = step_pos[0]
    number_of_steps = positions.shape[0]
    lengths = trace_len[0]
    trace_ends = jnp.cumsum(lengths)
    starts = jnp.sum(
        jnp.where(trace_ends[None, :] <= positions[:, None], lengths[None, :], 0), axis=1
    )
    key_pos = lax.axis_index(DP_SEQ) * count_of_keys + jnp.arange(count_of_keys, dtype=jnp.int32)
    allowed = (key_pos[None, :] <= positions[:, None]) & (key_pos[None, :] >= starts[:, None])
    score_list = []
    for head_cluster in range(KEY_VALUE_HEADS):
        query_part = query_all[
            :,
            head_cluster
            * query_groups
            * HEAD_WIDTH : (head_cluster + 1)
            * query_groups
            * HEAD_WIDTH,
        ].reshape(number_of_steps * query_groups, HEAD_WIDTH)
        key_part = keys[0, :, head_cluster * HEAD_WIDTH : (head_cluster + 1) * HEAD_WIDTH]
        score_part = lax.dot_general(
            query_part, key_part, (((1,), (1,)), ((), ())), preferred_element_type=jnp.float32
        ) * HEAD_WIDTH ** (-0.5)
        score_part = score_part.reshape(number_of_steps, query_groups, count_of_keys)
        score_list.append(jnp.where(allowed[:, None, :], score_part, MASKED))
    scores = jnp.stack(score_list, axis=1).reshape(number_of_steps, QUERY_HEADS, count_of_keys)
    local_peak = jnp.max(scores, axis=2)
    heads_of_values = values[0].reshape(count_of_keys, KEY_VALUE_HEADS, HEAD_WIDTH)
    complete_weight_rows = jnp.where(
        allowed[:, None, :], jnp.exp(scores - local_peak[:, :, None]), 0.0
    )
    totals = jnp.sum(complete_weight_rows, axis=2)
    reduced_weight_rows = complete_weight_rows.astype(jnp.bfloat16).reshape(
        number_of_steps, KEY_VALUE_HEADS, query_groups, count_of_keys
    )
    weighted = jnp.einsum(
        "skgt,tkd->skgd", reduced_weight_rows, heads_of_values, preferred_element_type=jnp.float32
    ).reshape(number_of_steps, QUERY_HEADS, HEAD_WIDTH)
    totals_hi, totals_lo = split_pair(totals)
    peak_hi, peak_lo = split_pair(local_peak)
    packed = jnp.concatenate(
        [
            weighted.astype(jnp.bfloat16),
            totals_hi[..., None],
            totals_lo[..., None],
            peak_hi[..., None],
            peak_lo[..., None],
        ],
        axis=-1,
    )
    arrived = lax.all_to_all(
        packed.reshape(1, *packed.shape), DP_SEQ, split_axis=2, concat_axis=0, tiled=True
    )
    attn = merge_heads(
        arrived[..., :HEAD_WIDTH].astype(jnp.float32),
        join_pair(arrived[..., HEAD_WIDTH], arrived[..., HEAD_WIDTH + 1]),
        join_pair(arrived[..., HEAD_WIDTH + 2], arrived[..., HEAD_WIDTH + 3]),
    )
    mixed = sent_and_summed(
        jnp.dot(attn, out_proj, preferred_element_type=jnp.float32).astype(jnp.bfloat16), DP_SEQ, 0
    )
    stream = residual[0].astype(jnp.float32) + mixed
    normed = (stream * rms_scale(stream) * norm_gain.astype(jnp.float32)[None, :]).astype(
        jnp.bfloat16
    )
    normed_all = lax.all_gather(normed, ROWS, axis=0, tiled=True)
    experts = router.shape[1]
    logits = jnp.dot(normed_all, router, preferred_element_type=jnp.float32)
    chosen = (routes_all[:, :, None] == jnp.arange(experts, dtype=jnp.int32)[None, None, :]).astype(
        jnp.float32
    )
    picked = jnp.sum(chosen * logits[:, None, :], axis=2)
    gate_weight = jax.nn.softmax(picked, axis=-1)
    mine = routes_all == lax.axis_index(DP_EXPERT)
    coef = jnp.sum(jnp.where(mine, gate_weight, 0.0), axis=1)
    gate_act = jnp.dot(normed_all, w_gate[0], preferred_element_type=jnp.float32)
    up_act = jnp.dot(normed_all, w_up[0], preferred_element_type=jnp.float32)
    hidden = (jax.nn.silu(gate_act) * up_act).astype(jnp.bfloat16)
    expert_out = jnp.dot(hidden, w_down[0], preferred_element_type=jnp.float32)
    expert_mix = lax.psum_scatter(coef[:, None] * expert_out, ROWS, scatter_dimension=0, tiled=True)
    final = stream + expert_mix
    reward, pull = jax.vjp(lambda value: head_logit(value, head_vec), final)
    target = labels[0].astype(jnp.float32)
    loss_term = jax.nn.softplus(reward) - target * reward
    logit_grad = jax.nn.sigmoid(reward) - target
    (final_grad,) = pull(logit_grad)
    d_mix = final_grad.astype(jnp.bfloat16)
    d_mix_all = lax.all_gather(d_mix, ROWS, axis=0, tiled=True)
    d_mix_wide = d_mix_all.astype(jnp.float32)
    contract_rows = (((0,), (0,)), ((), ()))
    d_out = (coef[:, None] * d_mix_wide).astype(jnp.bfloat16)
    grad_down = lax.dot_general(hidden, d_out, contract_rows, preferred_element_type=jnp.float32)
    grad_down = grad_down.astype(jnp.bfloat16).reshape((1,) + grad_down.shape)
    share_dot = jnp.sum(d_mix_wide * expert_out, axis=1)
    row_count = normed_all.shape[0]
    own_row = jnp.arange(row_count, dtype=jnp.int32) == lax.axis_index(ROWS)
    payload = jnp.concatenate(
        [jnp.where(mine, share_dot[:, None], 0.0), jnp.where(own_row, loss_term, 0.0)[:, None]],
        axis=1,
    )
    summed = lax.psum(payload, ROWS)
    route_dot = summed[:, :-1]
    loss = jnp.sum(summed[:, -1])
    pick_grad = gate_weight * (route_dot - jnp.sum(gate_weight * route_dot, axis=1, keepdims=True))
    d_logits = jnp.sum(chosen * pick_grad[:, :, None], axis=1)
    router_grad_all = lax.dot_general(
        normed_all.astype(jnp.float32), d_logits, contract_rows, precision=lax.Precision.HIGHEST
    )
    own_rows = router_grad_all.shape[0] // lax.axis_size(DP_SEQ_EXPERT)
    grad_router = lax.dynamic_slice_in_dim(
        router_grad_all, lax.axis_index(DP_SEQ_EXPERT) * own_rows, own_rows, axis=0
    ).astype(jnp.bfloat16)
    return (loss, grad_down, grad_router)


def solution(mesh):
    finer = Mesh(
        mesh.devices.reshape(mesh.shape["dp"], 2, 2, 4, 4),
        ("dp", "seq_0", "seq_1", "expert_0", "expert_1"),
    )
    return jax.shard_map(
        shards,
        mesh=finer,
        in_specs=(
            P(EXPERT, DP_SEQ, None),
            P(EXPERT, DP_SEQ, None),
            P(EXPERT, DP_SEQ, None),
            P(EXPERT, DP_SEQ, None),
            P(DP_SEQ, None),
            P(),
            P(),
            P(DP_EXPERT, None, SEQ),
            P(DP_EXPERT, None, SEQ),
            P(DP_EXPERT, SEQ, None),
            P(),
            P(EXPERT, "dp", None),
            P(EXPERT, None),
            P(EXPERT, DP_SEQ),
            P(EXPERT, None),
        ),
        out_specs=(P(), P(DP_EXPERT, SEQ, None), P(DP_SEQ_EXPERT, None)),
        check_vma=False,
    )
```

profile of v0, /device:TPU:1, one launch (start us, length us, event | category | flops | bytes accessed | tf_op | source)
XLA Modules:
  0.0 3206.8 jit_solution(4722802899857417348)
XLA Ops:
  7.2 0.8 reduce.14
  8.1 0.5 broadcast_in_dim.130
  8.5 0.5 broadcast.181
  9.0 2.2 reduce.15
  11.3 0.9 reshape.490
  12.1 16.7 all-to-all-start
  29.0 0.2 reduce-window.8
  29.3 18.7 all-to-all-done
  48.0 0.3 reshape.491
  48.3 0.3 copy.193
  48.7 0.2 fusion.13
  49.3 0.2 fusion.16
  49.5 0.2 fusion.30
  49.7 0.4 fusion.23
  50.4 0.3 copy.161
  50.7 0.3 copy.162
  51.0 0.3 fusion.8
  51.5 0.3 copy.163
  51.8 0.3 copy.164
  52.1 0.6 concatenate.6
  52.7 0.3 copy.165
  53.0 32.4 %all_to_all.28 = bf16[1,32,32,132]{3,1,0,2:T(8,128)(2,1)S(1)} all-to-all(bf16[1,32,32,132]{3,1,0,2:T(8,128)(2,1)S(1)} %copy.165), channel_id=1, replica_groups=mesh['dp'=8,'seq_0'=2,'seq_1'=2,'expert_0'=4,'expert_1'=4] {'dp','seq_0'..., dimensions={2} | all-to-all | bytes 540672 | tf_op jit(solution)/shard_map/all_to_all | solution.py:149
  85.4 1.1 copy.166
  86.6 0.5 multiply_reduce_fusion
  87.1 0.2 fusion.3
  87.3 0.7 reduce.16
  88.0 0.7 reshape.492
  88.7 9.7 all-to-all-start.2
  98.5 15.2 all-to-all-done.2
  113.8 0.2 convert_reduce_fusion
  114.0 0.6 copy-done.9
  114.6 0.6 multiply_reduce_fusion.5
  115.9 0.6 multiply_convert_fusion
  116.6 462.9 %all_gather.9 = s32[128,4,8]{2,1,0:T(4,128)S(1)} all-gather(s32[1,4,8]{2,1,0:T(4,128)S(1)} %copy-done.17), channel_id=1, replica_groups=mesh['dp'=8,'seq_0'=2,'seq_1'=2,'expert_0'=4,'expert_1'=4] {'dp','expert..., dimensions={0}, use_global_device_ids=true | all-gather | bytes 16512 | tf_op jit(solution)/shard_map/all_gather | solution.py:91
  580.0 0.5 copy-done.5
  580.5 593.1 %all-gather.5.cloned.1.call-done = bf16[1048576]{0:T(1024)(128)(2,1)} async-done(((bf16[2048]{0:T(1024)(128)(2,1)}), bf16[1048576]{0:T(1024)(128)(2,1)}) %all-gather.5.cloned.1.call-update) | async-done | bytes 2097168 | tf_op jit(solution)/shard_map/all_gather | solution.py:164
  1173.6 2.8 reshape.484
  1176.4 2.8 fusion.21
  1179.2 0.7 fusion.51
  1179.9 7.3 select_reduce_fusion.1
  1187.3 0.8 reduce_max.32
  1188.1 1.4 sub.91
  1189.4 1.3 fusion.45
  1190.7 1.4 div.48
  1192.1 1.3 copy.173
  1193.4 0.8 copy.171
  1194.2 0.7 copy.170
  1194.9 0.9 select_reduce_fusion.2
  1195.9 2.1 fusion.7
  1198.0 4.1 broadcast_multiply_fusion
  1202.2 0.6 copy-done.15
  1203.5 480.3 %all-reduce.3.cloned.1.call-done = f32[512,2048]{1,0:T(8,128)} async-done(((f32[512,2048]{1,0:T(8,128)}), f32[512,2048]{1,0:T(8,128)}) %all-reduce.3.cloned.1.call-update) | async-done | bytes 4194320
  1683.8 1.5 multiply_reduce_fusion.4
  1686.0 0.6 multiply_reduce_fusion.3
  1687.3 0.6 multiply_reduce_fusion.2
  1688.6 0.6 fusion.47
  1693.2 1384.5 %all-gather.7.cloned.1.call-done = bf16[512,1,2048]{2,1,0:T(2,128)(2,1)} async-done(((bf16[1,1,2048]{2,1,0:T(2,128)(2,1)}), bf16[512,1,2048]{2,1,0:T(2,128)(2,1)}) %all-gather.7.cloned.1.call-update) | async-done | bytes 2097168 | tf_op jit(solution)/shard_map/all_gather | solution.py:186
  3077.8 4.8 fusion
  3082.6 106.9 %psum.7 = f32[512,9]{0,1:T(8,128)S(1)} all-reduce(f32[512,9]{0,1:T(8,128)S(1)} %pad_maximum_fusion.2), channel_id=1, replica_groups=mesh['dp'=8,'seq_0'=2,'seq_1'=2,'expert_0'=4,'expert_1'=4] {'dp','seq_0'..., use_global_device_ids=true, to_apply=%region_18.19 | all-reduce | flops 4608 | bytes 36864 | tf_op jit(solution)/shard_map/psum | solution.py:199
  3189.6 0.6 slice_reduce_fusion
  3190.3 2.5 select_reduce_fusion
  3192.8 2.3 fusion.52
  3195.1 0.6 dynamic-slice_convert_fusion
  3195.7 4.6 fusion.2
  (81 shorter events, 2.4 us)
Async XLA Ops:
  7.2 1190.9 %copy-start = (bf16[1,192,2048]{2,1,0:T(8,128)(2,1)S(1)}, bf16[1,192,2048]{2,1,0:T(8,128)(2,1)}, u32[]{:S(2)}) copy-start(bf16[1,192,2048]{2,1,0:T(8,128)(2,1)} %param.24) | copy-start | bytes 2359300
  7.2 21.7 copy-start.8
  7.2 21.8 copy-start.19
  7.2 22.0 copy-start.18
  9.0 39.7 %copy-start.7 = (bf16[1,128,512]{2,1,0:T(8,128)(2,1)S(1)}, bf16[1,128,512]{2,1,0:T(8,128)(2,1)}, u32[]{:S(2)}) copy-start(bf16[1,128,512]{2,1,0:T(8,128)(2,1)} %param.15) | copy-start | bytes 393220
  12.1 35.9 %all-to-all-start = ((bf16[32,2,2048]{2,1,0:T(2,128)(2,1)}), bf16[32,2,2048]{2,1,0:T(2,128)(2,1)S(1)}, u32[]{:S(2)}, u32[]{:S(2)}) async-start(bf16[32,2,2048]{2,1,0:T(2,128)(2,1)} %reshape.490), calls=%async_computation | async-start | bytes 524288 | tf_op jit(solution)/shard_map/all_to_all | solution.py:28
  53.0 34.1 %copy-start.1 = (bf16[128,2048]{1,0:T(8,128)(2,1)S(1)}, bf16[128,2048]{1,0:T(8,128)(2,1)}, u32[]{:S(2)}) copy-start(bf16[128,2048]{1,0:T(8,128)(2,1)} %param.19) | copy-start | bytes 1572868
  85.3 13.1 copy-start.13
  86.5 29.4 copy-start.16
  86.5 30.1 copy-start.17
  88.7 25.0 all-to-all-start.2
  98.4 1075.2 %all-gather.5.cloned.1.call-start = ((), (), s32[]{:S(2)}) async-start(), calls=%async_computation.3 | async-start | bytes 2101248 | tf_op jit(solution)/shard_map/all_gather | solution.py:164
  114.0 0.6 copy-start.9
  116.5 1567.2 %all-reduce.3.cloned.1.call-start = ((), (), s32[]{:S(2)}) async-start(), calls=%async_computation.5 | async-start | bytes 8388608
  579.9 0.6 copy-start.5
  1176.4 2.8 copy-start.2
  1198.0 4.1 copy-start.3
  1202.1 0.7 copy-start.15
  1202.1 481.7 %copy-start.10 = (f32[2048]{0:T(1024)S(1)}, f32[2048]{0:T(1024)}, u32[]{:S(2)}) copy-start(f32[2048]{0:T(1024)} %copy-done.9) | copy-start | bytes 24580
  1202.1 481.7 %copy-start.14 = (bf16[1,1,2048]{2,1,0:T(2,128)(2,1)S(1)}, bf16[1,1,2048]{2,1,0:T(2,128)(2,1)}, u32[]{:S(2)}) copy-start(bf16[1,1,2048]{2,1,0:T(2,128)(2,1)} %param.18) | copy-start | bytes 12292
  1202.2 1875.6 %all-gather.7.cloned.1.call-start = ((), (), s32[]{:S(2)}) async-start(), calls=%async_computation.4 | async-start | bytes 4202496 | tf_op jit(solution)/shard_map/all_gather | solution.py:186
  3077.8 4.8 copy-start.6
  3077.8 111.8 %copy-start.11 = (f32[512]{0:T(512)S(1)}, f32[512]{0:T(512)}, u32[]{:S(2)}) copy-start(f32[512]{0:T(512)} %reduce_max.32) | copy-start | bytes 6148
  3077.8 111.8 %copy-start.12 = (f32[512]{0:T(512)S(1)}, f32[512]{0:T(512)}, u32[]{:S(2)}) copy-start(f32[512]{0:T(512)} %fusion.45) | copy-start | bytes 6148
  3190.3 5.4 copy-start.4
Sparse Core Ops, SparseCore 0:
  116.7 1056.8 all-gather.4
  1202.3 481.4 all-reduce.2
  1689.4 1388.3 all-gather.6
where the time goes:
time: 3210 us
  waiting for transfers between devices  2490 us (78%)
  blocking collectives  602 us (19%)
    all_gather x1, waiting for transfers between devices, shards(): d_mix_all = lax.all_gather(d_mix, ROWS, axis=0, tiled=True)  1380 us
    all_gather x1, waiting for transfers between devices, shards(): normed_all = lax.all_gather(normed, ROWS, axis=0, tiled=True)  593 us
    unnamed x4, waiting for transfers between devices  480 us
    all_gather x1, blocking collectives, shards(): block_routes = lax.all_gather(routes[0], DP_EXPERT, axis=0)  463 us
    psum x1, blocking collectives, shards(): summed = lax.psum(payload, ROWS)  107 us
  transfers between devices with their start and end apart: 5, of which 5 were waited for; matrix products, arithmetic and copies ran while one was open for 0% of the time, Pallas kernels for 0%

commit v1 on v0

--- a/solution.py
+++ b/solution.py
@@ -15,6 +15,12 @@
 ROWS = DP_SEQ_EXPERT
 MASKED = -1e30
 EPSILON = 1e-06
+
+
+def gather_and_add(x, axis):
+    terms = lax.all_gather(x, axis, axis=0, tiled=False)
+    total = terms.sum(axis=0)
+    return total
 
 
 def joined_along(blocks, dim):
@@ -196,7 +202,7 @@
         [jnp.where(mine, share_dot[:, None], 0.0), jnp.where(own_row, loss_term, 0.0)[:, None]],
         axis=1,
     )
-    summed = lax.psum(payload, ROWS)
+    summed = gather_and_add(payload, ROWS)
     route_dot = summed[:, :-1]
     loss = jnp.sum(summed[:, -1])
     pick_grad = gate_weight * (route_dot - jnp.sum(gate_weight * route_dot, axis=1, keepdims=True))

time: 3210 us -> 4550 us (1.42)
  waiting for transfers between devices: 2490 us -> 3920 us
  blocking collectives: 602 us -> 495 us
    all_gather x0 -> x1, waiting for transfers between devices: none -> 1430 us  [gather_and_add(): terms = lax.all_gather(x, axis, axis=0, tiled=False)]
    psum x1 -> x0, blocking collectives: 107 us -> none  [shards(): summed = lax.psum(payload, ROWS)]
    unnamed x4 -> x5, waiting for transfers between devices: 480 us -> 481 us
  transfers between devices with their start and end apart: 5 -> 6, of which waited for: 5 -> 6; matrix products, arithmetic and copies ran while one was open for 0% -> 0% of each run, Pallas kernels for 0% -> 0%
where the time goes in v1:
time: 4550 us
  waiting for transfers between devices  3920 us (86%)
  blocking collectives  495 us (11%)
    all_gather x1, waiting for transfers between devices, gather_and_add(): terms = lax.all_gather(x, axis, axis=0, tiled=False)  1430 us
    all_gather x1, waiting for transfers between devices, shards(): d_mix_all = lax.all_gather(d_mix, ROWS, axis=0, tiled=True)  1380 us
    all_gather x1, waiting for transfers between devices, shards(): normed_all = lax.all_gather(normed, ROWS, axis=0, tiled=True)  593 us
    unnamed x5, waiting for transfers between devices  481 us
    all_gather x1, blocking collectives, shards(): block_routes = lax.all_gather(routes[0], DP_EXPERT, axis=0)  463 us
  transfers between devices with their start and end apart: 6, of which 6 were waited for; matrix products, arithmetic and copies ran while one was open for 0% of the time, Pallas kernels for 0%

profile of v1, /device:TPU:1, one launch (start us, length us, event | category | flops | bytes accessed | tf_op | source)
XLA Modules:
  0.0 4548.4 jit_solution(8149939716975878739)
XLA Ops:
  7.2 0.8 reduce.14
  8.1 0.5 broadcast_in_dim.130
  8.5 0.5 broadcast.181
  9.0 2.2 reduce.15
  11.3 0.9 reshape.491
  12.1 16.7 all-to-all-start
  29.3 18.7 all-to-all-done
  48.0 0.3 reshape.492
  48.3 0.3 copy.195
  49.5 0.2 fusion.30
  49.8 0.4 fusion.23
  50.3 0.3 fusion.8
  50.8 0.3 copy.163
  51.1 0.3 copy.165
  51.4 0.3 copy.162
  51.8 0.3 copy.164
  52.1 0.5 concatenate.6
  52.6 0.3 copy.166
  52.9 32.4 all_to_all.28
  85.3 1.1 copy.167
  86.5 0.5 multiply_reduce_fusion
  87.0 0.2 fusion.3
  87.3 0.7 reduce.16
  88.0 0.7 reshape.493
  88.7 9.7 all-to-all-start.2
  98.5 15.2 all-to-all-done.2
  113.8 0.2 convert_reduce_fusion
  114.0 0.6 copy-done.7
  114.6 0.6 multiply_reduce_fusion.5
  115.9 0.6 multiply_convert_fusion
  116.6 462.9 %all_gather.15 = s32[128,4,8]{2,1,0:T(4,128)S(1)} all-gather(s32[1,4,8]{2,1,0:T(4,128)S(1)} %copy-done.15), channel_id=1, replica_groups=mesh['dp'=8,'seq_0'=2,'seq_1'=2,'expert_0'=4,'expert_1'=4] {'dp','expert..., dimensions={0}, use_global_device_ids=true | all-gather | bytes 16512 | tf_op jit(solution)/shard_map/all_gather | solution.py:97
  580.0 0.5 copy-done.3
  580.4 593.1 %all-gather.7.cloned.1.call-done = bf16[1048576]{0:T(1024)(128)(2,1)} async-done(((bf16[2048]{0:T(1024)(128)(2,1)}), bf16[1048576]{0:T(1024)(128)(2,1)}) %all-gather.7.cloned.1.call-update) | async-done | bytes 2097168 | tf_op jit(solution)/shard_map/all_gather | solution.py:170
  1173.5 2.8 reshape.484
  1176.4 1.8 fusion.51
  1178.1 7.3 select_reduce_fusion.1
  1185.5 0.8 reduce_max.32
  1186.3 1.4 sub.91
  1187.6 1.3 fusion.45
  1188.9 1.4 div.48
  1190.3 1.3 copy.174
  1191.6 1.3 copy.171
  1192.9 0.8 copy.172
  1193.7 1.0 select_reduce_fusion.2
  1194.8 2.0 fusion.21
  1196.9 0.9 fusion.7
  1197.7 4.1 broadcast_multiply_fusion
  1202.6 480.6 %all-reduce.3.cloned.1.call-done = f32[512,2048]{1,0:T(8,128)} async-done(((f32[512,2048]{1,0:T(8,128)}), f32[512,2048]{1,0:T(8,128)}) %all-reduce.3.cloned.1.call-update) | async-done | bytes 4194320
  1683.2 1.5 multiply_reduce_fusion.4
  1685.4 0.6 multiply_reduce_fusion.3
  1686.7 0.6 multiply_reduce_fusion.2
  1688.0 0.6 fusion.47
  1688.6 0.3 all-gather.9.cloned.1.call-start
  1692.9 1384.3 %all-gather.11.cloned.1.call-done = bf16[512,1,2048]{2,1,0:T(2,128)(2,1)} async-done(((bf16[1,1,2048]{2,1,0:T(2,128)(2,1)}), bf16[512,1,2048]{2,1,0:T(2,128)(2,1)}) %all-gather.11.cloned.1.call-update) | async-done | bytes 2097168 | tf_op jit(solution)/shard_map/all_gather | solution.py:192
  3077.2 4.8 fusion
  3082.0 0.6 pad_maximum_fusion.2
  3082.6 4.6 fusion.2
  3087.2 1432.3 %all-gather.9.cloned.1.call-done = f32[262144,9]{0,1:T(8,128)} async-done(((f32[512,9]{0,1:T(8,128)}), f32[262144,9]{0,1:T(8,128)}) %all-gather.9.cloned.1.call-update) | async-done | bytes 9437200 | tf_op jit(solution)/shard_map/all_gather | solution.py:21
  4519.5 15.2 copy.185
  4534.7 0.9 bitcast_reduce_fusion
  4535.6 0.6 slice_reduce_fusion
  4536.4 2.5 select_reduce_fusion
  4538.9 2.3 fusion.52
  4541.2 0.6 dynamic-slice_convert_fusion
  (83 shorter events, 2.9 us)
Async XLA Ops:
  7.2 1190.6 %copy-start = (bf16[1,192,2048]{2,1,0:T(8,128)(2,1)S(1)}, bf16[1,192,2048]{2,1,0:T(8,128)(2,1)}, u32[]{:S(2)}) copy-start(bf16[1,192,2048]{2,1,0:T(8,128)(2,1)} %param.24) | copy-start | bytes 2359300
  7.2 21.7 copy-start.6
  7.2 21.8 copy-start.17
  7.2 22.0 copy-start.16
  9.0 39.7 copy-start.5
  12.1 35.9 all-to-all-start
  52.9 34.1 copy-start.2
  85.3 13.1 copy-start.11
  86.4 29.4 copy-start.14
  86.5 30.1 copy-start.15
  88.7 25.0 all-to-all-start.2
  98.4 1075.2 %all-gather.7.cloned.1.call-start = ((), (), s32[]{:S(2)}) async-start(), calls=%async_computation.3 | async-start | bytes 2101248 | tf_op jit(solution)/shard_map/all_gather | solution.py:170
  114.0 0.6 copy-start.7
  116.5 1566.6 %all-reduce.3.cloned.1.call-start = ((), (), s32[]{:S(2)}) async-start(), calls=%async_computation.6 | async-start | bytes 8388608
  579.8 0.6 copy-start.3
  1194.8 2.1 copy-start.18
  1201.8 0.7 copy-start.13
  1201.8 481.4 %copy-start.8 = (f32[2048]{0:T(1024)S(1)}, f32[2048]{0:T(1024)}, u32[]{:S(2)}) copy-start(f32[2048]{0:T(1024)} %copy-done.7) | copy-start | bytes 24580
  1201.8 481.4 %copy-start.12 = (bf16[1,1,2048]{2,1,0:T(2,128)(2,1)S(1)}, bf16[1,1,2048]{2,1,0:T(2,128)(2,1)}, u32[]{:S(2)}) copy-start(bf16[1,1,2048]{2,1,0:T(2,128)(2,1)} %param.18) | copy-start | bytes 12292
  1201.8 1875.3 %all-gather.11.cloned.1.call-start = ((), (), s32[]{:S(2)}) async-start(), calls=%async_computation.5 | async-start | bytes 4202496 | tf_op jit(solution)/shard_map/all_gather | solution.py:192
  1688.6 2830.8 %all-gather.9.cloned.1.call-start = ((), (), s32[]{:S(2)}) async-start(), calls=%async_computation.4 | async-start | bytes 16809984 | tf_op jit(solution)/shard_map/all_gather | solution.py:21
  3077.2 4.8 copy-start.4
  4534.7 1.6 copy-start.9
  4534.7 1.6 copy-start.10
  4534.7 7.1 copy-start.1
Sparse Core Ops, SparseCore 0:
  116.6 1056.8 all-gather.6
  1202.0 481.1 all-reduce.2
  1688.8 1388.3 all-gather.10
  3082.7 1436.6 all-gather.8
